TPU v7x, 256 devices: a whole 4x4x8 slice. The times are simulated.
256 devices in a mesh: blk: 8 (over x, y_hi), batch: 32 (over y_lo, z, core).
Axes of the slice: x: 4, y: 4 (y_hi: 2, y_lo: 2; y = y_hi * 2 + y_lo), z: 8, core: 2. Of those that a mesh axis runs over, the one named last changes fastest.
Arguments:
- frame_one: bfloat16 [32, 4096, 128], P('batch', 'blk'), may hold values from -40 to 40
- frame_two: bfloat16 [32, 4096, 128], P('batch', 'blk'), may hold values from -40 to 40
- encoder_weight: bfloat16 [128, 256], replicated, may hold values from -0.5 to 0.5
- flow_grad: float32 [32, 2, 4096], P('batch', None, 'blk'), may hold values from -6 to 6
Outputs:
- flow: float32 [32, 2, 4096], P('batch', None, 'blk')
- grad_w: float32 [128, 256], replicated
All inputs are finite; a program needn't handle non-finite values.
Results may differ from a plain program's by a relative error of at most 0.01.
Values may be sent and summed in bfloat16 or wider, within the bound.
No kernel may reach another device: no remote copies, remote signals or barrier semaphores. Data moves between devices by JAX's collectives and lax.ppermute only.
A program may use at most 64 MiB of HBM per device.

v0:
```python
import jax
import jax.numpy as jnp
from jax import lax
from jax.sharding import PartitionSpec as P

WIDTH = 240


def grid_coords(start, count):
    position = start + jnp.arange(count, dtype=jnp.int32)
    col_coord = (position % WIDTH).astype(jnp.float32) / 64.0
    row_coord = (position // WIDTH).astype(jnp.float32) / 8.0
    return (col_coord, row_coord)


def body(frame_one, frame_two, encoder_weight, flow_grad):
    first_in = frame_one[0]
    second_in = frame_two[0]
    grad_col = flow_grad[0, 0]
    grad_row = flow_grad[0, 1]
    query_count = first_in.shape[0]
    channels = encoder_weight.shape[1]
    scaling = channels ** (-0.5)
    first_feat = jnp.dot(first_in, encoder_weight, preferred_element_type=jnp.float32).astype(
        jnp.bfloat16
    )
    second_feat = jnp.dot(second_in, encoder_weight, preferred_element_type=jnp.float32).astype(
        jnp.bfloat16
    )
    own_col, own_row = grid_coords(lax.axis_index("blk") * query_count, query_count)
    zero_rows = jnp.zeros((query_count,), jnp.float32)
    forward_run_max = jnp.full((query_count,), -jnp.inf, jnp.float32)
    forward_run_sum = zero_rows
    sum_col = zero_rows
    sum_row = zero_rows
    key_feat = lax.all_gather(second_feat, "blk", axis=0, tiled=True)
    logits = scaling * jnp.dot(first_feat, key_feat.T, preferred_element_type=jnp.float32)
    key_col, key_row = grid_coords(jnp.int32(0), key_feat.shape[0])
    new_max = jnp.max(logits, axis=1)
    rescale = jnp.exp(forward_run_max - new_max)
    expo = jnp.exp(logits - new_max[:, None])
    forward_run_sum = forward_run_sum * rescale + jnp.sum(expo, axis=1)
    sum_col = sum_col * rescale + jnp.sum(expo * key_col[None, :], axis=1)
    sum_row = sum_row * rescale + jnp.sum(expo * key_row[None, :], axis=1)
    stats = (new_max, forward_run_sum, sum_col, sum_row)
    run_max, run_sum, sum_col, sum_row = stats
    mean_col = sum_col / run_sum
    mean_row = sum_row / run_sum
    inner = grad_col * mean_col + grad_row * mean_row
    flow = jnp.stack([mean_col - own_col, mean_row - own_row])[None]
    key_feat = lax.all_gather(second_feat, "blk", axis=0, tiled=True)
    logits = scaling * jnp.dot(first_feat, key_feat.T, preferred_element_type=jnp.float32)
    probs = jnp.exp(logits - run_max[:, None]) / run_sum[:, None]
    key_col, key_row = grid_coords(jnp.int32(0), key_feat.shape[0])
    slope = (
        probs
        * (
            grad_col[:, None] * key_col[None, :]
            + grad_row[:, None] * key_row[None, :]
            - inner[:, None]
        )
    ).astype(jnp.bfloat16)
    first_accum = jnp.dot(slope, key_feat, preferred_element_type=jnp.float32)
    first_accum, slope_store = (first_accum, slope)
    delta_one = (scaling * first_accum).astype(jnp.bfloat16)
    local_grad = jnp.dot(first_in.T, delta_one, preferred_element_type=jnp.float32)
    delta_two = lax.psum_scatter(
        scaling * jnp.dot(slope_store.T, first_feat, preferred_element_type=jnp.float32),
        "blk",
        scatter_dimension=0,
        tiled=True,
    )
    second_term = jnp.dot(
        second_in.astype(jnp.float32).T,
        delta_two,
        precision=lax.Precision.HIGHEST,
        preferred_element_type=jnp.float32,
    )
    local_grad = local_grad + second_term
    grad_w = lax.psum(local_grad, ("blk", "batch"))
    return (flow, grad_w)


def solution(mesh):
    placed = (P("batch", "blk", None), P("batch", "blk", None), P(), P("batch", None, "blk"))
    return jax.shard_map(
        body, mesh=mesh, in_specs=placed, out_specs=(P("batch", None, "blk"), P()), check_vma=False
    )
```

profile of v0, /device:TPU:2, one launch (start us, length us, event | category | flops | bytes accessed | tf_op | source)
XLA Modules:
  0.0 437.6 jit_solution(4563758125745906845)
XLA Ops:
  7.2 0.0 copy-start
  7.2 0.0 all-gather.2.cloned.1.call-start
  7.2 1.8 convolution_convert_fusion
  9.1 0.0 all-gather.2.cloned.1.call-update
  9.1 0.0 reduce-scatter.2.cloned.1.call-start
  9.2 0.8 fusion.24
  9.9 0.0 copy-done
  9.9 1.0 convolution_convert_fusion.1
  11.0 62.5 %all-gather.2.cloned.1.call-done = bf16[4096,256]{1,0:T(8,128)(2,1)} async-done(((bf16[512,256]{1,0:T(8,128)(2,1)}), bf16[4096,256]{1,0:T(8,128)(2,1)}) %all-gather.2.cloned.1.call-update) | async-done | bytes 2097168 | tf_op jit(solution)/shard_map/all_gather | solution.py:36
  73.5 3.0 multiply_reduce_fusion.2
  76.5 3.1 multiply_reduce_fusion.1
  79.6 4.2 multiply_convert_fusion
  83.8 0.0 copy-start.1
  83.8 1.9 copy-done.1
  85.7 0.0 copy-start.2
  85.7 3.3 convolution_multiply_fusion
  89.0 0.0 copy-start.3
  89.0 0.0 reduce-scatter.2.cloned.1.call-update
  89.0 0.0 all-reduce.2.cloned.1.call-start
  89.1 0.0 copy-done.2
  89.1 3.7 fusion.2
  92.9 85.5 %reduce-scatter.2.cloned.1.call-done = f32[512,256]{1,0:T(8,128)} async-done(((f32[4096,256]{1,0:T(8,128)}), f32[512,256]{1,0:T(8,128)}) %reduce-scatter.2.cloned.1.call-update) | async-done | bytes 524304 | tf_op jit(solution)/shard_map/reduce_scatter | solution.py:67
  178.4 0.0 copy-done.3
  178.4 2.3 fusion.1
  180.7 0.0 all-reduce.2.cloned.1.call-update
  180.7 0.6 maximum_bitcast_fusion
  181.3 248.1 %all-reduce.2.cloned.1.call-done = f32[128,256]{0,1:T(8,128)} async-done(((f32[128,256]{0,1:T(8,128)}), f32[128,256]{0,1:T(8,128)}) %all-reduce.2.cloned.1.call-update) | async-done | bytes 131088 | tf_op jit(solution)/shard_map/psum | solution.py:80
  429.4 1.7 copy.6
  (4 shorter events, 0.1 us)
Async XLA Ops:
  7.2 2.8 copy-start
  7.2 66.3 %all-gather.2.cloned.1.call-start = ((), (), s32[]{:S(2)}) async-start(), calls=%async_computation.1 | async-start | bytes 2359296 | tf_op jit(solution)/shard_map/all_gather | solution.py:36
  9.1 169.3 %reduce-scatter.2.cloned.1.call-start = ((), (), s32[]{:S(2)}) async-start(), calls=%async_computation.2 | async-start | bytes 4718592 | tf_op jit(solution)/shard_map/reduce_scatter | solution.py:67
  83.8 1.9 copy-start.1
  85.7 3.4 copy-start.2
  89.0 89.4 %copy-start.3 = (bf16[1,512,128]{2,1,0:T(8,128)(2,1)S(1)}, bf16[1,512,128]{2,1,0:T(8,128)(2,1)}, u32[]{:S(2)}) copy-start(bf16[1,512,128]{2,1,0:T(8,128)(2,1)} %param.5) | copy-start | bytes 393220
  89.0 340.4 %all-reduce.2.cloned.1.call-start = ((), (), s32[]{:S(2)}) async-start(), calls=%async_computation.3 | async-start | bytes 262144 | tf_op jit(solution)/shard_map/psum | solution.py:80
Sparse Core Ops, SparseCore 0:
  10.6 62.8 all-gather.1
  89.1 89.2 reduce-scatter.1
  184.5 244.9 all-reduce.1
where the time goes:
time: 438 us
  waiting for transfers between devices  396 us (90%)
  matrix products  15.1 us (3%)
  between operations  13.8 us (3%)
  other arithmetic  7.96 us (2%)
  local copies, waits for them, and re-layouts  4.38 us (1%)
    psum x1, waiting for transfers between devices, body(): grad_w = lax.psum(local_grad, ('blk', 'batch'))  248 us
    reduce_scatter x1, waiting for transfers between devices, body(): lax.psum_scatter(scaling * jnp.dot(slope_store.T, first_feat, preferred_e...  85.5 us
    all_gather x1, waiting for transfers between devices, body(): key_feat = lax.all_gather(second_feat, 'blk', axis=0, tiled=True)  62.5 us
  transfers between devices with their start and end apart: 3, of which 3 were waited for; matrix products, arithmetic and copies ran while one was open for 1% of the time, Pallas kernels for 0%

commit v1 on v0

--- a/solution.py
+++ b/solution.py
@@ -77,7 +77,8 @@
         preferred_element_type=jnp.float32,
     )
     local_grad = local_grad + second_term
-    grad_w = lax.psum(local_grad, ("blk", "batch"))
+    piece_now = lax.all_gather(local_grad, ("blk", "batch"))
+    grad_w = jnp.sum(piece_now, 0)
     return (flow, grad_w)
 
 

time: 438 us -> 392 us (0.89)
  waiting for transfers between devices: 396 us -> 329 us
  local copies, waits for them, and re-layouts: 4.38 us -> 20.7 us
    psum x1 -> x0, waiting for transfers between devices: 248 us -> none  [body(): grad_w = lax.psum(local_grad, ('blk', 'batch'))]
    all_gather x0 -> x1, waiting for transfers between devices: none -> 181 us  [body(): piece_now = lax.all_gather(local_grad, ('blk', 'batch'))]
    unnamed x9 -> x12, local copies, waits for them, and re-layouts: 3.61 us -> 19.9 us
  transfers between devices with their start and end apart: 3 -> 3, of which waited for: 3 -> 3; matrix products, arithmetic and copies ran while one was open for 1% -> 2% of each run, Pallas kernels for 0% -> 0%
where the time goes in v1:
time: 392 us; the launch traced here: 390 us
  waiting for transfers between devices  329 us (84%)
  local copies, waits for them, and re-layouts  20.7 us (5%)
  matrix products  15.1 us (4%)
  between operations  13.8 us (4%)
  other arithmetic  12 us (3%)
    all_gather x1, waiting for transfers between devices, body(): piece_now = lax.all_gather(local_grad, ('blk', 'batch'))  181 us
    reduce_scatter x1, waiting for transfers between devices, body(): lax.psum_scatter(scaling * jnp.dot(slope_store.T, first_feat, preferred_e...  85.6 us
    all_gather x1, waiting for transfers between devices, body(): key_feat = lax.all_gather(second_feat, 'blk', axis=0, tiled=True)  62.5 us
    unnamed x12, local copies, waits for them, and re-layouts  19.9 us
  transfers between devices with their start and end apart: 3, of which 3 were waited for; matrix products, arithmetic and copies ran while one was open for 2% of the time, Pallas kernels for 0%

profile of v1, /device:TPU:2, one launch (start us, length us, event | category | flops | bytes accessed | tf_op | source)
XLA Modules:
  0.0 390.4 jit_solution(12148507394453188477)
XLA Ops:
  7.2 0.0 copy-start
  7.2 0.0 all-gather.4.cloned.1.call-start
  7.2 1.8 convolution_convert_fusion
  9.1 0.0 all-gather.4.cloned.1.call-update
  9.1 0.0 reduce-scatter.2.cloned.1.call-start
  9.2 0.8 fusion.24
  9.9 0.0 copy-done
  9.9 1.0 convolution_convert_fusion.1
  11.0 62.5 %all-gather.4.cloned.1.call-done = bf16[4096,256]{1,0:T(8,128)(2,1)} async-done(((bf16[512,256]{1,0:T(8,128)(2,1)}), bf16[4096,256]{1,0:T(8,128)(2,1)}) %all-gather.4.cloned.1.call-update) | async-done | bytes 2097168 | tf_op jit(solution)/shard_map/all_gather | solution.py:36
  73.5 3.0 multiply_reduce_fusion.2
  76.5 3.1 multiply_reduce_fusion.1
  79.6 4.2 %multiply_convert_fusion = bf16[512,4096]{1,0:T(8,128)(2,1)S(1)} fusion(f32[512]{0:T(512)S(1)} %get-tuple-element.7, f32[512]{0:T(512)S(1)} %bitcast.36, f32[512]{0:T(512)S(1)} %bitcast.34, f32[512]{0:T(512)S(1)} %get-tuple-element.10, f32[4096]{0:T(1024)S(1)} %get-tuple-element.15, f32[4096]{0:T(1024)S(1)} %get-tuple-element.16, ...), kind=kLoop, calls=%fused_computation.1 | loop fusion | flops 18874368 | bytes 12625920 | tf_op jit(solution)/shard_map/convert_element_type | solution.py:62
  83.8 0.0 copy-start.2
  83.8 1.9 copy-done.2
  85.7 0.0 copy-start.3
  85.7 3.2 convolution_multiply_fusion
  89.0 0.0 copy-start.4
  89.0 0.0 reduce-scatter.2.cloned.1.call-update
  89.0 0.0 all-gather.6.cloned.1.call-start
  89.0 0.0 copy-done.3
  89.1 3.7 fusion.2
  92.8 85.6 %reduce-scatter.2.cloned.1.call-done = f32[512,256]{1,0:T(8,128)} async-done(((f32[4096,256]{1,0:T(8,128)}), f32[512,256]{1,0:T(8,128)}) %reduce-scatter.2.cloned.1.call-update) | async-done | bytes 524304 | tf_op jit(solution)/shard_map/reduce_scatter | solution.py:67
  178.4 0.0 copy-done.4
  178.4 2.3 fusion.1
  180.7 0.0 all-gather.6.cloned.1.call-update
  180.8 0.6 maximum_bitcast_fusion
  181.4 180.5 %all-gather.6.cloned.1.call-done = f32[32768,256]{0,1:T(8,128)} async-done(((f32[128,256]{0,1:T(8,128)}), f32[32768,256]{0,1:T(8,128)}) %all-gather.6.cloned.1.call-update) | async-done | bytes 33554448 | tf_op jit(solution)/shard_map/all_gather | solution.py:80
  361.9 17.2 %copy.7 = f32[32,8,256,128]{3,2,1,0:T(8,128)S(1)} copy(f32[32,8,256,128]{3,1,2,0:T(8,128)} %bitcast.32) | data formatting | bytes 67108864
  379.1 0.0 copy-start.1
  379.2 4.0 %bitcast_reduce_fusion = f32[128,256]{0,1:T(8,128)S(1)} fusion(f32[32,8,256,128]{3,2,1,0:T(8,128)S(1)} %copy.7), kind=kLoop, calls=%fused_computation | loop fusion | flops 8355840 | bytes 33685504 | tf_op jit(solution)/shard_map/reduce_sum | solution.py:81
  383.2 0.8 copy.6
  383.9 0.0 copy-done.1
  (4 shorter events, 0.1 us)
Async XLA Ops:
  7.2 2.8 copy-start
  7.2 66.3 %all-gather.4.cloned.1.call-start = ((), (), s32[]{:S(2)}) async-start(), calls=%async_computation.1 | async-start | bytes 2359296 | tf_op jit(solution)/shard_map/all_gather | solution.py:36
  9.1 169.3 %reduce-scatter.2.cloned.1.call-start = ((), (), s32[]{:S(2)}) async-start(), calls=%async_computation.2 | async-start | bytes 4718592 | tf_op jit(solution)/shard_map/reduce_scatter | solution.py:67
  83.8 1.9 copy-start.2
  85.7 3.3 copy-start.3
  89.0 89.4 %copy-start.4 = (bf16[1,512,128]{2,1,0:T(8,128)(2,1)S(1)}, bf16[1,512,128]{2,1,0:T(8,128)(2,1)}, u32[]{:S(2)}) copy-start(bf16[1,512,128]{2,1,0:T(8,128)(2,1)} %param.5) | copy-start | bytes 393220
  89.0 272.9 %all-gather.6.cloned.1.call-start = ((), (), s32[]{:S(2)}) async-start(), calls=%async_computation.3 | async-start | bytes 33685504 | tf_op jit(solution)/shard_map/all_gather | solution.py:80
  379.1 4.8 %copy-start.1 = (bf16[1,512,128]{2,1,0:T(8,128)(2,1)S(1)}, bf16[1,512,128]{2,1,0:T(8,128)(2,1)}, u32[]{:S(2)}) copy-start(bf16[1,512,128]{2,1,0:T(8,128)(2,1)} %param.4) | copy-start | bytes 393220
Sparse Core Ops, SparseCore 0:
  10.6 62.8 all-gather.3
  89.1 89.2 reduce-scatter.1
  182.8 179.0 all-gather.5
